TPU v7x, 256 devices: a whole 4x4x8 slice. The times are simulated.
256 devices in a mesh: dp: 32 (over x, z), tensor: 8 (over y, core).
Axes of the slice: x: 4, y: 4, z: 8, core: 2. Of those that a mesh axis runs over, the one named last changes fastest.
Arguments:
- counts: int32 [32], replicated, may hold values from 1 to 32, 512 in all
- keys: bfloat16 [1024, 28672], P('dp'), may hold values from -6 to 6
- inverse_cov: bfloat16 [28672, 28672], P('tensor', 'dp'), as said below
- hidden: bfloat16 [1024, 8192], P('dp', 'tensor'), may hold values from -6 to 6
- targets: bfloat16 [1024, 8192], P('dp', 'tensor'), may hold values from -48 to 48
- down_weight: bfloat16 [8192, 28672], P('tensor', 'dp'), may hold values from -0.03125 to 0.03125
Outputs:
- new_weight: bfloat16 [8192, 28672], P('tensor', 'dp')
- next_resid: bfloat16 [1024, 8192], P('dp', 'tensor')
Inputs may be any that keep to these rules, and one draw needn't show every extreme that they name: Group g has counts[g] live edits in its first counts[g] slots; the counts sum to 512; some group holds 32. `inverse_cov`: symmetric positive definite.
All inputs are finite; a program needn't handle non-finite values.
Results may differ from a plain program's by a relative error of at most 0.01.
The roundings to bfloat16 on the way count: a program that leaves them out, or rounds other values in their place, can miss the bound.
Values may be sent and summed in bfloat16 or wider, within the bound.
No kernel may reach another device: no remote copies, remote signals or barrier semaphores. Data moves between devices by JAX's collectives and lax.ppermute only.
A program may use at most 128 MiB of HBM per device.

v0:
```python
import jax
import jax.numpy as jnp
from jax import lax
from jax.sharding import PartitionSpec as P

LAYERS_LEFT = 3


def cholesky_solve(system, right_side):
    factor = jnp.linalg.cholesky(system)
    middle = lax.linalg.triangular_solve(factor, right_side, left_side=True, lower=True)
    return lax.linalg.triangular_solve(factor, middle, left_side=True, lower=True, transpose_a=True)


def rows_product(left, right):
    return lax.dot_general(
        left, right, (((1,), (1,)), ((), ())), preferred_element_type=jnp.float32
    )


def pick(select, values):
    return jnp.dot(select, values, preferred_element_type=jnp.float32).astype(values.dtype)


def gather_rows(x, axis):
    n = lax.axis_size(axis)
    copies = jnp.broadcast_to(x[None], (n,) + x.shape)
    return lax.all_to_all(copies, axis, 0, 0, tiled=True).reshape((n * x.shape[0],) + x.shape[1:])


def scatter_rows_sum(x, axis):
    n = lax.axis_size(axis)
    parts = lax.all_to_all(x.reshape((n, x.shape[0] // n) + x.shape[1:]), axis, 0, 0, tiled=True)
    return parts.sum(0)


def per_device(counts, keys, inverse_cov, hidden, targets, down_weight):
    slot_count = keys.shape[0]
    group_size = lax.axis_size("dp")
    group_index = lax.axis_index("dp")
    tensor_index = lax.axis_index("tensor")
    width_part = inverse_cov.shape[0]
    row_total = slot_count * group_size
    live_total = row_total // 2
    ends = jnp.cumsum(counts)
    starts = ends - counts
    compact = jnp.arange(live_total, dtype=jnp.int32)
    owner = jnp.minimum(jnp.sum(compact[:, None] >= ends[None, :], axis=1), group_size - 1)
    row_of = owner * slot_count + compact - starts[owner]
    select = (row_of[:, None] == jnp.arange(row_total, dtype=jnp.int32)[None, :]).astype(
        jnp.bfloat16
    )
    slots = jnp.arange(slot_count, dtype=jnp.int32)
    live_vec = slots < counts[group_index]
    live_slot = live_vec[:, None]
    own_compact = jnp.where(live_vec, starts[group_index] + slots, 0)
    masked_keys = jnp.where(live_slot, keys, jnp.zeros_like(keys))
    column_part = lax.dynamic_slice_in_dim(masked_keys, tensor_index * width_part, width_part, 1)
    columns = lax.all_to_all(masked_keys, "dp", split_axis=1, concat_axis=0, tiled=True)
    gathered = lax.all_gather(column_part, "dp", axis=0, tiled=True)
    change = (targets.astype(jnp.float32) - hidden.astype(jnp.float32)) / LAYERS_LEFT
    resid_local = jnp.where(live_slot, change, jnp.zeros_like(change)).astype(jnp.bfloat16)
    gathered, columns = lax.optimization_barrier((gathered, columns))
    resid_all = lax.all_gather(resid_local, "dp", axis=0, tiled=True)
    keys_c = pick(select, gathered)
    columns_c = pick(select, columns)
    partial_q = jnp.dot(keys_c, inverse_cov, preferred_element_type=jnp.float32)
    tensor_size = lax.axis_size("tensor")
    parts_q = (
        lax.all_to_all(
            partial_q.astype(jnp.bfloat16).reshape((tensor_size, -1) + partial_q.shape[1:]),
            "tensor",
            0,
            0,
            tiled=True,
        )
        .astype(jnp.float32)
        .sum(0)
    )
    precond_c = gather_rows(parts_q.astype(jnp.bfloat16), "tensor")
    gram_c = gather_rows(scatter_rows_sum(rows_product(precond_c, columns_c), "dp"), "dp")
    base_partial = rows_product(columns, down_weight)
    gram_c, base_partial = lax.optimization_barrier((gram_c, base_partial))
    base = scatter_rows_sum(base_partial, "dp")
    system = gram_c + jnp.eye(live_total, dtype=jnp.float32)
    factor = jnp.linalg.cholesky(system)
    factor, resid_all = lax.optimization_barrier((factor, resid_all))
    resid_c = pick(select, resid_all)
    middle = lax.linalg.triangular_solve(
        factor, resid_c.astype(jnp.float32), left_side=True, lower=True
    )
    solved_c = lax.linalg.triangular_solve(
        factor, middle, left_side=True, lower=True, transpose_a=True
    ).astype(jnp.bfloat16)
    weight_delta = lax.dot_general(
        solved_c, precond_c, (((0,), (0,)), ((), ())), preferred_element_type=jnp.float32
    )
    new_weight = (down_weight.astype(jnp.float32) + weight_delta).astype(jnp.bfloat16)
    gram_own = jnp.where(live_slot, jnp.take(gram_c, own_compact, axis=1).T, 0.0)
    extra = jnp.dot(
        gram_own,
        solved_c.astype(jnp.float32),
        precision=lax.Precision.HIGHEST,
        preferred_element_type=jnp.float32,
    )
    summed = hidden.astype(jnp.float32) + (base + extra)
    next_resid = jnp.where(live_slot, summed, jnp.zeros_like(summed)).astype(jnp.bfloat16)
    return (new_weight, next_resid)


def solution(mesh):
    in_specs = (
        P(),
        P("dp", None),
        P("tensor", "dp"),
        P("dp", "tensor"),
        P("dp", "tensor"),
        P("tensor", "dp"),
    )
    out_specs = (P("tensor", "dp"), P("dp", "tensor"))
    return jax.shard_map(
        per_device, mesh=mesh, in_specs=in_specs, out_specs=out_specs, check_vma=False
    )
```

profile of v0, /device:TPU:2, one launch (start us, length us, event | category | flops | bytes accessed | tf_op | source)
XLA Modules:
  0.0 408.6 jit_solution(1317642860902086746)
XLA Ops:
  12.9 11.7 %all-to-all-start = ((bf16[32,32,896]{2,0,1:T(8,128)(2,1)}), bf16[32,32,896]{2,0,1:T(8,128)(2,1)S(1)}, u32[]{:S(2)}, u32[]{:S(2)}) async-start(bf16[32,32,896]{2,0,1:T(8,128)(2,1)} %bitcast.127), calls=%async_computation | async-start | bytes 3670016 | tf_op jit(solution)/shard_map/all_to_all | solution.py:59
  26.4 4.4 %compare_select_fusion.1 = (s32[512,1]{0,1:T(1,128)S(1)}, s32[512,1]{0,1:T(1,128)S(1)}) fusion(s32[]{:T(128)} %bitcast.27, s32[]{:T(128)} %bitcast.28, s32[]{:T(128)} %bitcast.29, s32[]{:T(128)} %bitcast.30, s32[]{:T(128)} %bitcast.31, s32[]{:T(128)} %bitcast.33, s32[]{:T(128)} %bitcast.32, s32[512,1]{0,1:T(1,128)S(1)} %bitcast.136), kind=kLoop, calls=%fused_computation.136 | loop fusion | flops 7680 | bytes 6172 | tf_op jit(solution)/shard_map/gather | solution.py:49
  31.0 15.8 %select_subtract_fusion = s32[512]{0:T(512)S(1)} fusion(pred[512]{0:T(512)(128)(4,1)S(1)} %get-tuple-element.46, pred[512]{0:T(512)(128)(4,1)S(1)} %get-tuple-element.45, pred[512]{0:T(512)(128)(4,1)S(1)} %get-tuple-element.44, pred[512]{0:T(512)(128)(4,1)S(1)} %get-tuple-element.43, pred[512]{0:T(512)(128)(4,1)S(1)} %get-tuple-element.42, ...), kind=kLoop, calls=%fused_computation.145 | loop fusion | flops 14848 | bytes 19044 | tf_op jit(solution)/shard_map/sub | solution.py:49
  46.8 28.5 %all-to-all-done = bf16[32,32,896]{2,0,1:T(8,128)(2,1)S(1)} async-done(((bf16[32,32,896]{2,0,1:T(8,128)(2,1)}), bf16[32,32,896]{2,0,1:T(8,128)(2,1)S(1)}, u32[]{:S(2)}, u32[]{:S(2)}) %all-to-all-start) | async-done | bytes 1835040 | tf_op jit(solution)/shard_map/all_to_all | solution.py:59
  75.4 41.5 %all-gather.3.cloned.1.call-done = bf16[1024,3584]{1,0:T(8,128)(2,1)} async-done(((bf16[32,3584]{1,0:T(8,128)(2,1)}), bf16[1024,3584]{1,0:T(8,128)(2,1)}) %all-gather.3.cloned.1.call-update) | async-done | bytes 7340048 | tf_op jit(solution)/shard_map/all_gather | solution.py:60
  116.9 13.7 %convolution_convert_fusion.1 = bf16[512,896]{1,0:T(8,128)(2,1)} fusion(bf16[3584,896]{1,0:T(8,128)(2,1)} %param.8, bf16[1024,3584]{1,0:T(8,128)(2,1)} %all-gather.3.cloned.1.call-done, s32[512]{0:T(512)S(1)} %select_subtract_fusion), kind=kOutput, calls=%fused_computation.24 | convolution fusion | flops 7049248768 | bytes 14682112 | tf_op jit(solution)/shard_map/dot_general | solution.py:67
  130.5 18.9 %all_to_all.44 = bf16[8,64,896]{2,1,0:T(8,128)(2,1)S(1)} all-to-all(bf16[8,64,896]{2,1,0:T(8,128)(2,1)} %bitcast.134), channel_id=1, replica_groups=mesh['dp'=32,'tensor'=8] {'tensor'}, dimensions={0} | all-to-all | bytes 1835008 | tf_op jit(solution)/shard_map/all_to_all | solution.py:70
  149.6 17.7 %all_to_all.45 = bf16[8,64,896]{2,1,0:T(8,128)(2,1)} all-to-all(bf16[8,64,896]{2,1,0:T(8,128)(2,1)S(1)} %broadcast_in_dim.72), channel_id=1, replica_groups=mesh['dp'=32,'tensor'=8] {'tensor'}, dimensions={0} | all-to-all | bytes 1835008 | tf_op jit(solution)/shard_map/all_to_all | solution.py:28
  167.3 3.0 fusion.37
  170.3 33.0 %all_to_all.46 = f32[32,16,512]{2,1,0:T(8,128)S(1)} all-to-all(f32[32,16,512]{2,1,0:T(8,128)S(1)} %fusion.37), channel_id=1, replica_groups=mesh['dp'=32,'tensor'=8] {'dp'}, dimensions={0} | all-to-all | bytes 2097152 | tf_op jit(solution)/shard_map/all_to_all | solution.py:33
  204.5 7.5 %all-to-all-start.4 = ((f32[32,16,512]{2,1,0:T(8,128)}), f32[32,16,512]{2,1,0:T(8,128)S(1)}, u32[]{:S(2)}, u32[]{:S(2)}) async-start(f32[32,16,512]{2,1,0:T(8,128)} %broadcast_in_dim.73), calls=%async_computation.4 | async-start | bytes 2097152 | tf_op jit(solution)/shard_map/all_to_all | solution.py:28
  216.7 6.3 %fusion.88 = f32[1024,1024]{1,0:T(8,128)} fusion(bf16[1024,896]{1,0:T(8,128)(2,1)} %bitcast.131, bf16[1024,896]{1,0:T(8,128)(2,1)} %param.11), kind=kOutput, calls=%fused_computation.176 | convolution fusion | flops 1879048192 | bytes 7864320 | tf_op jit(solution)/shard_map/dot_general | solution.py:16
  223.0 15.5 %all-to-all-done.4 = f32[32,16,512]{2,1,0:T(8,128)S(1)} async-done(((f32[32,16,512]{2,1,0:T(8,128)}), f32[32,16,512]{2,1,0:T(8,128)S(1)}, u32[]{:S(2)}, u32[]{:S(2)}) %all-to-all-start.4) | async-done | bytes 1048608 | tf_op jit(solution)/shard_map/all_to_all | solution.py:28
  239.5 11.7 %cholesky.104 = f32[128,128]{1,0:T(8,128)S(1)} custom-call(f32[128,128]{1,0:T(8,128)S(1)} %cholesky.266), custom_call_target="Cholesky" | custom-call | tf_op jit(solution)/shard_map/jit(cholesky)/cholesky | solution.py:86
  251.4 9.8 %custom-call.32 = f32[1,128,128]{1,2,0:T(8,128)S(1)} custom-call(f32[1,128,128]{2,1,0:T(8,128)S(1)} %get-tuple-element.68), custom_call_target="InvertDiagBlocksLowerTriangular" | custom-call | tf_op jit(solution)/shard_map/jit(cholesky)/cholesky | solution.py:86
  261.9 12.1 %cholesky.217 = f32[128,128]{1,0:T(8,128)S(1)} custom-call(f32[128,128]{1,0:T(8,128)S(1)} %cholesky.270), custom_call_target="Cholesky" | custom-call | tf_op jit(solution)/shard_map/jit(cholesky)/cholesky | solution.py:86
  274.0 7.7 %all-to-all-start.5 = ((f32[32,32,1024]{2,1,0:T(8,128)}), f32[32,32,1024]{2,1,0:T(8,128)}, u32[]{:S(2)}, u32[]{:S(2)}) async-start(f32[32,32,1024]{2,1,0:T(8,128)} %bitcast.128), calls=%async_computation.5 | async-start | bytes 8388608 | tf_op jit(solution)/shard_map/all_to_all | solution.py:33
  281.7 9.8 %custom-call.33 = f32[1,128,128]{1,2,0:T(8,128)S(1)} custom-call(f32[1,128,128]{2,1,0:T(8,128)S(1)} %get-tuple-element.65), custom_call_target="InvertDiagBlocksLowerTriangular" | custom-call | tf_op jit(solution)/shard_map/jit(cholesky)/cholesky | solution.py:86
  292.2 11.7 %cholesky.238 = f32[128,128]{1,0:T(8,128)S(1)} custom-call(f32[128,128]{1,0:T(8,128)S(1)} %cholesky.275), custom_call_target="Cholesky" | custom-call | tf_op jit(solution)/shard_map/jit(cholesky)/cholesky | solution.py:86
  303.9 9.8 %custom-call.34 = f32[1,128,128]{1,2,0:T(8,128)S(1)} custom-call(f32[1,128,128]{2,1,0:T(8,128)S(1)} %get-tuple-element.62), custom_call_target="InvertDiagBlocksLowerTriangular" | custom-call | tf_op jit(solution)/shard_map/jit(cholesky)/cholesky | solution.py:86
  314.3 11.9 %cholesky.255 = f32[128,128]{1,0:T(8,128)S(1)} custom-call(f32[128,128]{1,0:T(8,128)S(1)} %convolution_subtract_fusion.6), custom_call_target="Cholesky" | custom-call | tf_op jit(solution)/shard_map/jit(cholesky)/cholesky | solution.py:86
  331.5 10.4 %while.1 = (s32[]{:T(128)}, f32[512,512]{1,0:T(8,128)S(1)}, s32[4,2]{0,1:T(2,128)S(1)}, f32[4,128,128]{2,1,0:T(8,128)}, s32[]{:T(128)}) while((s32[]{:T(128)}, f32[512,512]{1,0:T(8,128)S(1)}, s32[4,2]{0,1:T(2,128)S(1)}, f32[4,128,128]{2,1,0:T(8,128)}, s32[]{:T(128)}) %tuple.97), condition=%wide.while_cond, body=%wide.while_body.sunk | while | flops 2 | bytes 132705 | solution.py:92
  341.9 40.1 %custom-call.35 = f32[4,128,128]{1,2,0:T(8,128)S(1)} custom-call(f32[4,128,128]{2,1,0:T(8,128)} %get-tuple-element.21), custom_call_target="InvertDiagBlocksLowerTriangular" | custom-call | tf_op jit(solution)/shard_map/triangular_solve | solution.py:92
  382.7 2.9 fusion.84
  (104 shorter events, 46.3 us)
Async XLA Ops:
  7.2 109.7 %all-gather.3.cloned.1.call-start = ((), (), s32[]{:S(2)}) async-start(), calls=%async_computation.6 | async-start | bytes 7569408 | tf_op jit(solution)/shard_map/all_gather | solution.py:60
  9.0 203.3 %copy-start.4 = (pred[32]{0:T(512)(128)(4,1)}, pred[32]{0:T(512)(128)(4,1)S(1)}, u32[]{:S(2)}) copy-start(pred[32]{0:T(512)(128)(4,1)S(1)} %iota_compare_fusion.19) | copy-start | bytes 100
  12.9 11.8 %copy-start.6 = (s32[32]{0:T(128)S(1)}, s32[32]{0:T(128)}, u32[]{:S(2)}) copy-start(s32[32]{0:T(128)} %param.6) | copy-start | bytes 388
  12.9 62.5 %all-to-all-start = ((bf16[32,32,896]{2,0,1:T(8,128)(2,1)}), bf16[32,32,896]{2,0,1:T(8,128)(2,1)S(1)}, u32[]{:S(2)}, u32[]{:S(2)}) async-start(bf16[32,32,896]{2,0,1:T(8,128)(2,1)} %bitcast.127), calls=%async_computation | async-start | bytes 3670016 | tf_op jit(solution)/shard_map/all_to_all | solution.py:59
  75.4 91.9 %copy-start = (bf16[32,32,896]{2,0,1:T(8,128)(2,1)}, bf16[32,32,896]{2,0,1:T(8,128)(2,1)S(1)}, u32[]{:S(2)}) copy-start(bf16[32,32,896]{2,0,1:T(8,128)(2,1)S(1)} %all-to-all-done) | copy-start | bytes 5505028
  203.3 9.0 %copy-start.2 = (bf16[32,1024]{1,0:T(8,128)(2,1)S(1)}, bf16[32,1024]{1,0:T(8,128)(2,1)}, u32[]{:S(2)}) copy-start(bf16[32,1024]{1,0:T(8,128)(2,1)} %param.10) | copy-start | bytes 196612
  203.4 9.0 %copy-start.3 = (bf16[32,1024]{1,0:T(8,128)(2,1)S(1)}, bf16[32,1024]{1,0:T(8,128)(2,1)}, u32[]{:S(2)}) copy-start(bf16[32,1024]{1,0:T(8,128)(2,1)} %param.9) | copy-start | bytes 196612
  204.5 33.9 %all-to-all-start.4 = ((f32[32,16,512]{2,1,0:T(8,128)}), f32[32,16,512]{2,1,0:T(8,128)S(1)}, u32[]{:S(2)}, u32[]{:S(2)}) async-start(f32[32,16,512]{2,1,0:T(8,128)} %broadcast_in_dim.73), calls=%async_computation.4 | async-start | bytes 2097152 | tf_op jit(solution)/shard_map/all_to_all | solution.py:28
  212.1 119.0 %all-gather.5.cloned.1.call-start = ((), (), s32[]{:S(2)}) async-start(), calls=%async_computation.7 | async-start | bytes 2162688 | tf_op jit(solution)/shard_map/all_gather | solution.py:64
  274.0 123.9 %all-to-all-start.5 = ((f32[32,32,1024]{2,1,0:T(8,128)}), f32[32,32,1024]{2,1,0:T(8,128)}, u32[]{:S(2)}, u32[]{:S(2)}) async-start(f32[32,32,1024]{2,1,0:T(8,128)} %bitcast.128), calls=%async_computation.5 | async-start | bytes 8388608 | tf_op jit(solution)/shard_map/all_to_all | solution.py:33
  330.9 0.7 copy-start.9
  393.5 1.7 copy-start.1
  393.5 1.8 copy-start.7
  397.8 2.4 copy-start.5
  397.8 2.5 copy-start.8
Sparse Core Ops, SparseCore 0:
  11.6 105.2 all-gather.2
  216.1 81.9 all-gather.4
where the time goes:
time: 417 us; the launch traced here: 409 us
  other arithmetic  150 us (36%)
  waiting for transfers between devices  85.5 us (21%)
  blocking collectives  69.6 us (17%)
  matrix products  41.2 us (10%)
  starting transfers between devices  27.2 us (7%)
  local copies, waits for them, and re-layouts  18.3 us (4%)
  between operations  17.3 us (4%)
    another operation x14, other arithmetic, per_device(): factor = jnp.linalg.cholesky(system)  79 us
    all_gather x1, waiting for transfers between devices, per_device(): gathered = lax.all_gather(column_part, 'dp', axis=0, tiled=True)  41.5 us
    another operation x3, other arithmetic, per_device(): lax.linalg.triangular_solve(factor, middle, left_side=True, lower=True, t...  40.8 us
    all_to_all x1, blocking collectives, scatter_rows_sum(): lax.all_to_all(x.reshape((n, x.shape[0] // n) + x.shape[1:]), axis, 0, 0,...  33 us
    all_to_all x1, waiting for transfers between devices, per_device(): lax.all_to_all(masked_keys, 'dp', split_axis=1, concat_axis=0, tiled=True)  28.5 us
    all_to_all x1, blocking collectives, per_device(): lax.all_to_all(partial_q.astype(jnp.bfloat16).reshape((tensor_size, -1) +...  18.9 us
    all_to_all x1, blocking collectives, gather_rows(): lax.all_to_all(copies, axis, 0, 0, tiled=True)  17.7 us
    sub x1, other arithmetic, per_device(): row_of = owner * slot_count + compact - starts[owner]  15.8 us
  transfers between devices with their start and end apart: 5, of which 3 were waited for; matrix products, arithmetic and copies ran while one was open for 45% of the time, Pallas kernels for 0%

commit v1 on v0

--- a/solution.py
+++ b/solution.py
@@ -57,7 +57,9 @@
     masked_keys = jnp.where(live_slot, keys, jnp.zeros_like(keys))
     column_part = lax.dynamic_slice_in_dim(masked_keys, tensor_index * width_part, width_part, 1)
     columns = lax.all_to_all(masked_keys, "dp", split_axis=1, concat_axis=0, tiled=True)
-    gathered = lax.all_gather(column_part, "dp", axis=0, tiled=True)
+    gathered = jnp.concatenate(
+        lax.all_to_all(jnp.stack([column_part] * lax.axis_size("dp")), "dp", 0, 0), axis=0
+    )
     change = (targets.astype(jnp.float32) - hidden.astype(jnp.float32)) / LAYERS_LEFT
     resid_local = jnp.where(live_slot, change, jnp.zeros_like(change)).astype(jnp.bfloat16)
     gathered, columns = lax.optimization_barrier((gathered, columns))

time: 417 us -> 542 us (1.30)
  waiting for transfers between devices: 85.5 us -> 197 us
  starting transfers between devices: 27.2 us -> 35.7 us
    all_to_all x0 -> x1, waiting for transfers between devices: none -> 139 us  [per_device(): lax.all_to_all(jnp.stack([column_part] * lax.axis_size('dp')), 'dp', 0, 0)]
    all_gather x1 -> x0, waiting for transfers between devices: 41.5 us -> none  [per_device(): gathered = lax.all_gather(column_part, 'dp', axis=0, tiled=True)]
    all_to_all x1, waiting for transfers between devices: 28.5 us -> 42.2 us  [per_device(): lax.all_to_all(masked_keys, 'dp', split_axis=1, concat_axis=0, tiled=True)]
    all_to_all x0 -> x1, starting transfers between devices: none -> 8.61 us  [per_device(): lax.all_to_all(jnp.stack([column_part] * lax.axis_size('dp')), 'dp', 0, 0)]
    another operation x13 -> x14, local copies, waits for them, and re-layouts: 10.5 us -> 14.3 us
  transfers between devices with their start and end apart: 5 -> 5, of which waited for: 3 -> 3; matrix products, arithmetic and copies ran while one was open for 45% -> 34% of each run, Pallas kernels for 0% -> 0%
where the time goes in v1:
time: 542 us; the launch traced here: 533 us
  waiting for transfers between devices  197 us (36%)
  other arithmetic  150 us (28%)
  blocking collectives  71.7 us (13%)
  matrix products  40.9 us (8%)
  starting transfers between devices  35.7 us (7%)
  local copies, waits for them, and re-layouts  21.6 us (4%)
  between operations  17.2 us (3%)
    all_to_all x1, waiting for transfers between devices, per_device(): lax.all_to_all(jnp.stack([column_part] * lax.axis_size('dp')), 'dp', 0, 0)  139 us
    another operation x14, other arithmetic, per_device(): factor = jnp.linalg.cholesky(system)  78.9 us
    all_to_all x1, waiting for transfers between devices, per_device(): lax.all_to_all(masked_keys, 'dp', split_axis=1, concat_axis=0, tiled=True)  42.2 us
    another operation x3, other arithmetic, per_device(): lax.linalg.triangular_solve(factor, middle, left_side=True, lower=True, t...  40.8 us
    all_to_all x1, blocking collectives, scatter_rows_sum(): lax.all_to_all(x.reshape((n, x.shape[0] // n) + x.shape[1:]), axis, 0, 0,...  35.9 us
    all_to_all x1, blocking collectives, per_device(): lax.all_to_all(partial_q.astype(jnp.bfloat16).reshape((tensor_size, -1) +...  18.8 us
    all_to_all x1, blocking collectives, gather_rows(): lax.all_to_all(copies, axis, 0, 0, tiled=True)  17 us
    sub x1, other arithmetic, per_device(): row_of = owner * slot_count + compact - starts[owner]  15.5 us
  transfers between devices with their start and end apart: 5, of which 3 were waited for; matrix products, arithmetic and copies ran while one was open for 34% of the time, Pallas kernels for 0%

profile of v1, /device:TPU:2, one launch (start us, length us, event | category | flops | bytes accessed | tf_op | source)
XLA Modules:
  0.0 533.5 jit_solution(11980158027452281120)
XLA Ops:
  12.2 11.7 %all-to-all-start.1 = ((bf16[32,32,896]{2,0,1:T(8,128)(2,1)}), bf16[32,32,896]{2,0,1:T(8,128)(2,1)}, u32[]{:S(2)}, u32[]{:S(2)}) async-start(bf16[32,32,896]{2,0,1:T(8,128)(2,1)} %bitcast.128), calls=%async_computation.1 | async-start | bytes 3670016 | tf_op jit(solution)/shard_map/all_to_all | solution.py:59
  23.9 42.2 %all-to-all-done.1 = bf16[32,32,896]{2,0,1:T(8,128)(2,1)} async-done(((bf16[32,32,896]{2,0,1:T(8,128)(2,1)}), bf16[32,32,896]{2,0,1:T(8,128)(2,1)}, u32[]{:S(2)}, u32[]{:S(2)}) %all-to-all-start.1) | async-done | bytes 1835040 | tf_op jit(solution)/shard_map/all_to_all | solution.py:59
  66.1 3.9 stack.2
  69.9 8.6 %all-to-all-start = ((bf16[32,32,3584]{2,1,0:T(8,128)(2,1)}), bf16[32,32,3584]{2,1,0:T(8,128)(2,1)}, u32[]{:S(2)}, u32[]{:S(2)}) async-start(bf16[32,32,3584]{2,1,0:T(8,128)(2,1)} %stack.2), calls=%async_computation | async-start | bytes 14680064 | tf_op jit(solution)/shard_map/all_to_all | solution.py:61
  80.4 4.6 compare_select_fusion.1
  85.1 15.5 %select_subtract_fusion = s32[512]{0:T(512)S(1)} fusion(pred[512]{0:T(512)(128)(4,1)S(1)} %get-tuple-element.46, pred[512]{0:T(512)(128)(4,1)S(1)} %get-tuple-element.45, pred[512]{0:T(512)(128)(4,1)S(1)} %get-tuple-element.44, pred[512]{0:T(512)(128)(4,1)S(1)} %get-tuple-element.43, pred[512]{0:T(512)(128)(4,1)S(1)} %get-tuple-element.42, ...), kind=kLoop, calls=%fused_computation.145 | loop fusion | flops 14848 | bytes 19044 | tf_op jit(solution)/shard_map/sub | solution.py:49
  100.7 139.3 %all-to-all-done = bf16[32,32,3584]{2,1,0:T(8,128)(2,1)} async-done(((bf16[32,32,3584]{2,1,0:T(8,128)(2,1)}), bf16[32,32,3584]{2,1,0:T(8,128)(2,1)}, u32[]{:S(2)}, u32[]{:S(2)}) %all-to-all-start) | async-done | bytes 7340064 | tf_op jit(solution)/shard_map/all_to_all | solution.py:61
  240.0 12.7 %convolution_convert_fusion.1 = bf16[512,896]{1,0:T(8,128)(2,1)S(1)} fusion(bf16[3584,896]{1,0:T(8,128)(2,1)} %param.8, bf16[1024,3584]{1,0:T(8,128)(2,1)} %bitcast.36, s32[512]{0:T(512)S(1)} %select_subtract_fusion), kind=kOutput, calls=%fused_computation.24 | convolution fusion | flops 7049248768 | bytes 14682112 | tf_op jit(solution)/shard_map/dot_general | solution.py:69
  252.7 18.8 %all_to_all.49 = bf16[8,64,896]{2,1,0:T(8,128)(2,1)S(1)} all-to-all(bf16[8,64,896]{2,1,0:T(8,128)(2,1)S(1)} %bitcast.133), channel_id=1, replica_groups=mesh['dp'=32,'tensor'=8] {'tensor'}, dimensions={0} | all-to-all | bytes 1835008 | tf_op jit(solution)/shard_map/all_to_all | solution.py:72
  271.8 17.0 %all_to_all.50 = bf16[8,64,896]{2,1,0:T(8,128)(2,1)S(1)} all-to-all(bf16[8,64,896]{2,1,0:T(8,128)(2,1)S(1)} %broadcast_in_dim.72), channel_id=1, replica_groups=mesh['dp'=32,'tensor'=8] {'tensor'}, dimensions={0} | all-to-all | bytes 1835008 | tf_op jit(solution)/shard_map/all_to_all | solution.py:28
  292.5 35.9 %all_to_all.51 = f32[32,16,512]{2,1,0:T(8,128)S(1)} all-to-all(f32[32,16,512]{2,1,0:T(8,128)S(1)} %fusion.37), channel_id=1, replica_groups=mesh['dp'=32,'tensor'=8] {'dp'}, dimensions={0} | all-to-all | bytes 2097152 | tf_op jit(solution)/shard_map/all_to_all | solution.py:33
  329.6 7.5 %all-to-all-start.5 = ((f32[32,16,512]{2,1,0:T(8,128)}), f32[32,16,512]{2,1,0:T(8,128)S(1)}, u32[]{:S(2)}, u32[]{:S(2)}) async-start(f32[32,16,512]{2,1,0:T(8,128)} %broadcast_in_dim.73), calls=%async_computation.5 | async-start | bytes 2097152 | tf_op jit(solution)/shard_map/all_to_all | solution.py:28
  341.9 6.3 %fusion.88 = f32[1024,1024]{1,0:T(8,128)} fusion(bf16[1024,896]{1,0:T(8,128)(2,1)} %bitcast.38, bf16[1024,896]{1,0:T(8,128)(2,1)} %param.11), kind=kOutput, calls=%fused_computation.176 | convolution fusion | flops 1879048192 | bytes 7864320 | tf_op jit(solution)/shard_map/dot_general | solution.py:16
  348.3 15.2 %all-to-all-done.5 = f32[32,16,512]{2,1,0:T(8,128)S(1)} async-done(((f32[32,16,512]{2,1,0:T(8,128)}), f32[32,16,512]{2,1,0:T(8,128)S(1)}, u32[]{:S(2)}, u32[]{:S(2)}) %all-to-all-start.5) | async-done | bytes 1048608 | tf_op jit(solution)/shard_map/all_to_all | solution.py:28
  364.5 11.7 %cholesky.104 = f32[128,128]{1,0:T(8,128)S(1)} custom-call(f32[128,128]{1,0:T(8,128)S(1)} %cholesky.266), custom_call_target="Cholesky" | custom-call | tf_op jit(solution)/shard_map/jit(cholesky)/cholesky | solution.py:88
  376.4 9.8 %custom-call.32 = f32[1,128,128]{1,2,0:T(8,128)S(1)} custom-call(f32[1,128,128]{2,1,0:T(8,128)S(1)} %get-tuple-element.68), custom_call_target="InvertDiagBlocksLowerTriangular" | custom-call | tf_op jit(solution)/shard_map/jit(cholesky)/cholesky | solution.py:88
  386.9 12.1 %cholesky.217 = f32[128,128]{1,0:T(8,128)S(1)} custom-call(f32[128,128]{1,0:T(8,128)S(1)} %cholesky.270), custom_call_target="Cholesky" | custom-call | tf_op jit(solution)/shard_map/jit(cholesky)/cholesky | solution.py:88
  399.0 7.6 %all-to-all-start.6 = ((f32[32,32,1024]{2,1,0:T(8,128)}), f32[32,32,1024]{2,1,0:T(8,128)}, u32[]{:S(2)}, u32[]{:S(2)}) async-start(f32[32,32,1024]{2,1,0:T(8,128)} %bitcast.129), calls=%async_computation.6 | async-start | bytes 8388608 | tf_op jit(solution)/shard_map/all_to_all | solution.py:33
  406.7 9.8 %custom-call.33 = f32[1,128,128]{1,2,0:T(8,128)S(1)} custom-call(f32[1,128,128]{2,1,0:T(8,128)S(1)} %get-tuple-element.65), custom_call_target="InvertDiagBlocksLowerTriangular" | custom-call | tf_op jit(solution)/shard_map/jit(cholesky)/cholesky | solution.py:88
  417.2 11.7 %cholesky.238 = f32[128,128]{1,0:T(8,128)S(1)} custom-call(f32[128,128]{1,0:T(8,128)S(1)} %cholesky.275), custom_call_target="Cholesky" | custom-call | tf_op jit(solution)/shard_map/jit(cholesky)/cholesky | solution.py:88
  428.9 9.8 %custom-call.34 = f32[1,128,128]{1,2,0:T(8,128)S(1)} custom-call(f32[1,128,128]{2,1,0:T(8,128)S(1)} %get-tuple-element.62), custom_call_target="InvertDiagBlocksLowerTriangular" | custom-call | tf_op jit(solution)/shard_map/jit(cholesky)/cholesky | solution.py:88
  439.3 11.9 %cholesky.255 = f32[128,128]{1,0:T(8,128)S(1)} custom-call(f32[128,128]{1,0:T(8,128)S(1)} %convolution_subtract_fusion.6), custom_call_target="Cholesky" | custom-call | tf_op jit(solution)/shard_map/jit(cholesky)/cholesky | solution.py:88
  456.4 10.4 %while.1 = (s32[]{:T(128)}, f32[512,512]{1,0:T(8,128)S(1)}, s32[4,2]{0,1:T(2,128)S(1)}, f32[4,128,128]{2,1,0:T(8,128)}, s32[]{:T(128)}) while((s32[]{:T(128)}, f32[512,512]{1,0:T(8,128)S(1)}, s32[4,2]{0,1:T(2,128)S(1)}, f32[4,128,128]{2,1,0:T(8,128)}, s32[]{:T(128)}) %tuple.97), condition=%wide.while_cond, body=%wide.while_body.sunk | while | flops 2 | bytes 132205 | solution.py:94
  466.8 40.1 %custom-call.35 = f32[4,128,128]{1,2,0:T(8,128)S(1)} custom-call(f32[4,128,128]{2,1,0:T(8,128)} %get-tuple-element.21), custom_call_target="InvertDiagBlocksLowerTriangular" | custom-call | tf_op jit(solution)/shard_map/triangular_solve | solution.py:94
  (104 shorter events, 52.3 us)
Async XLA Ops:
  9.1 328.3 %copy-start.4 = (pred[32]{0:T(512)(128)(4,1)}, pred[32]{0:T(512)(128)(4,1)S(1)}, u32[]{:S(2)}) copy-start(pred[32]{0:T(512)(128)(4,1)S(1)} %iota_compare_fusion.19) | copy-start | bytes 100
  12.2 53.9 %all-to-all-start.1 = ((bf16[32,32,896]{2,0,1:T(8,128)(2,1)}), bf16[32,32,896]{2,0,1:T(8,128)(2,1)}, u32[]{:S(2)}, u32[]{:S(2)}) async-start(bf16[32,32,896]{2,0,1:T(8,128)(2,1)} %bitcast.128), calls=%async_computation.1 | async-start | bytes 3670016 | tf_op jit(solution)/shard_map/all_to_all | solution.py:59
  69.9 8.6 %copy-start.6 = (s32[32]{0:T(128)S(1)}, s32[32]{0:T(128)}, u32[]{:S(2)}) copy-start(s32[32]{0:T(128)} %param.6) | copy-start | bytes 388
  69.9 170.1 %all-to-all-start = ((bf16[32,32,3584]{2,1,0:T(8,128)(2,1)}), bf16[32,32,3584]{2,1,0:T(8,128)(2,1)}, u32[]{:S(2)}, u32[]{:S(2)}) async-start(bf16[32,32,3584]{2,1,0:T(8,128)(2,1)} %stack.2), calls=%async_computation | async-start | bytes 14680064 | tf_op jit(solution)/shard_map/all_to_all | solution.py:61
  288.8 3.7 copy-start
  328.4 9.0 %copy-start.2 = (bf16[32,1024]{1,0:T(8,128)(2,1)S(1)}, bf16[32,1024]{1,0:T(8,128)(2,1)}, u32[]{:S(2)}) copy-start(bf16[32,1024]{1,0:T(8,128)(2,1)} %param.10) | copy-start | bytes 196612
  328.4 9.0 %copy-start.3 = (bf16[32,1024]{1,0:T(8,128)(2,1)S(1)}, bf16[32,1024]{1,0:T(8,128)(2,1)}, u32[]{:S(2)}) copy-start(bf16[32,1024]{1,0:T(8,128)(2,1)} %param.9) | copy-start | bytes 196612
  329.6 33.9 %all-to-all-start.5 = ((f32[32,16,512]{2,1,0:T(8,128)}), f32[32,16,512]{2,1,0:T(8,128)S(1)}, u32[]{:S(2)}, u32[]{:S(2)}) async-start(f32[32,16,512]{2,1,0:T(8,128)} %broadcast_in_dim.73), calls=%async_computation.5 | async-start | bytes 2097152 | tf_op jit(solution)/shard_map/all_to_all | solution.py:28
  337.1 118.7 %all-gather.2.cloned.1.call-start = ((), (), s32[]{:S(2)}) async-start(), calls=%async_computation.7 | async-start | bytes 2162688 | tf_op jit(solution)/shard_map/all_gather | solution.py:66
  399.0 123.7 %all-to-all-start.6 = ((f32[32,32,1024]{2,1,0:T(8,128)}), f32[32,32,1024]{2,1,0:T(8,128)}, u32[]{:S(2)}, u32[]{:S(2)}) async-start(f32[32,32,1024]{2,1,0:T(8,128)} %bitcast.129), calls=%async_computation.6 | async-start | bytes 8388608 | tf_op jit(solution)/shard_map/all_to_all | solution.py:33
  455.7 0.7 copy-start.9
  518.3 1.7 copy-start.1
  518.3 1.8 copy-start.7
  522.7 2.4 copy-start.5
  522.7 2.5 copy-start.8
Sparse Core Ops, SparseCore 0:
  341.1 81.6 all-gather.1
